TPU v7x, 128 devices: a whole 4x4x4 slice. The times are simulated.
128 devices in a mesh: dp: 4 (over y_hi, core), head: 4 (over x), ctx: 8 (over z, y_lo).
Axes of the slice: x: 4, y: 4 (y_hi: 2, y_lo: 2; y = y_hi * 2 + y_lo), z: 4, core: 2. Of those that a mesh axis runs over, the one named last changes fastest.
Arguments:
- video: bfloat16 [16, 64, 24576], P('dp', 'head', 'ctx'), parts along dimension 0, may hold values from -6 to 6
- cache: bfloat16 [8, 64, 24576], P('dp', 'head', 'ctx'), parts along dimension 0, may hold values from -6 to 6
- conv_weight: bfloat16 [3, 3, 288, 192], replicated, may hold values from -0.125 to 0.125
- conv_bias: float32 [192], replicated, may hold values from -3 to 3
- down_weight: bfloat16 [768, 192], replicated, may hold values from -0.21875 to 0.21875
- patch_weight: bfloat16 [768, 5120], P(None, ('head', 'ctx')), may hold values from -0.21875 to 0.21875
- step_index: int32 [4], P('dp'), parts along dimension 0, may hold values from 0 to 999
- mod_weight: bfloat16 [256, 10240], P(None, ('head', 'ctx')), may hold values from -1 to 1
- qkv_weight: bfloat16 [5120, 20, 3, 128], P('ctx', 'head'), may hold values from -0.078125 to 0.078125
Outputs:
- attended: bfloat16 [16384, 2560], P(('dp', 'ctx'), 'head'), parts along dimension 0
There are 4 independent parts, one for each index of `dp`. A program takes and returns all parts, laid end to end along the dimension named above; an argument that names none is the same for every part. Nothing has to cross between parts.
All inputs are finite; a program needn't handle non-finite values.
Results may differ from a plain program's by a relative error of at most 0.015.
The roundings to bfloat16 on the way count: a program that leaves them out, or rounds other values in their place, can miss the bound.
Values may be sent and summed in bfloat16 or wider, within the bound.
No kernel may reach another device: no remote copies, remote signals or barrier semaphores. Data moves between devices by JAX's collectives and lax.ppermute only.
A program may use at most 128 MiB of HBM per device.

v0:
```python
import jax
import jax.numpy as jnp
from jax import lax
from jax.sharding import PartitionSpec as P

D = 5120
HDIM = 128
FREQ = 256


def with_halo(cells, sides, width):
    for axis, dim in sides:
        count = lax.axis_size(axis)
        ends = count - 1
        head = lax.slice_in_dim(cells, 0, width, axis=dim)
        tail = lax.slice_in_dim(cells, cells.shape[dim] - width, cells.shape[dim], axis=dim)
        cells = jnp.concatenate(
            [
                lax.ppermute(tail, axis, [(i, (i + 1) % count) for i in range(ends)]),
                cells,
                lax.ppermute(head, axis, [((i + 1) % count, i) for i in range(ends)]),
            ],
            axis=dim,
        )
    return cells


def silu_act(value):
    return value * jax.nn.sigmoid(value)


def shards(
    video,
    cache,
    conv_weight,
    conv_bias,
    down_weight,
    patch_weight,
    step_index,
    mod_weight,
    qkv_weight,
):
    cin = conv_weight.shape[2] // 3
    cmid = conv_weight.shape[3]
    frame_count = video.shape[0]
    tile_rows = video.shape[1]
    tile_cols = video.shape[2] // cin
    frames = jnp.concatenate([cache, video], 0).reshape(frame_count + 2, tile_rows, tile_cols, cin)
    padded = with_halo(frames, (("head", 1), ("ctx", 2)), 1)
    total = jnp.zeros((frame_count, tile_rows, tile_cols, cmid), jnp.float32)
    for time_tap in range(3):
        for row_tap in range(3):
            slab = padded[time_tap : time_tap + frame_count, row_tap : row_tap + tile_rows]
            stacked = jnp.concatenate(
                [slab[:, :, col_tap : col_tap + tile_cols] for col_tap in range(3)], -1
            )
            total = total + jnp.einsum(
                "fyxc,cd->fyxd",
                stacked,
                conv_weight[time_tap, row_tap],
                preferred_element_type=jnp.float32,
            )
    hidden = silu_act(total + conv_bias).astype(jnp.bfloat16)
    stacked = (
        hidden.reshape(frame_count, tile_rows // 2, 2, tile_cols // 2, 2, cmid)
        .transpose(0, 1, 3, 2, 4, 5)
        .reshape(-1, 4 * cmid)
    )
    reduced = silu_act(jnp.dot(stacked, down_weight, preferred_element_type=jnp.float32)).astype(
        jnp.bfloat16
    )
    reduced = reduced.reshape(frame_count, tile_rows // 2, tile_cols // 2, cmid)
    patches = reduced.reshape(frame_count, tile_rows // 4, 2, tile_cols // 4, 2, cmid).transpose(
        0, 1, 3, 2, 4, 5
    )
    patches = patches.reshape(-1, 4 * cmid)
    half = FREQ // 2
    freqs = jnp.exp(-jnp.log(10000.0) * jnp.arange(half, dtype=jnp.float32) / half)
    angles = step_index[0].astype(jnp.float32) * freqs
    timing = jnp.concatenate([jnp.cos(angles), jnp.sin(angles)]).astype(jnp.bfloat16)
    mod_share = jnp.dot(timing[None, :], mod_weight, preferred_element_type=jnp.float32)[0]
    modulation = lax.all_gather(mod_share, ("head", "ctx"), axis=0, tiled=True)
    scale = modulation[:D]
    shift = modulation[D:]
    embedded = jnp.dot(
        patches,
        lax.all_gather(patch_weight, ("head", "ctx"), axis=1, tiled=True),
        preferred_element_type=jnp.float32,
    )
    inverse = lax.rsqrt(jnp.mean(embedded * embedded, -1, keepdims=True) + 1e-06)
    normed = (embedded * inverse * (1.0 + scale) + shift).astype(jnp.bfloat16)
    gathered = lax.all_gather(normed, "head", axis=0, tiled=True)
    group_rows = gathered.shape[0]
    heads_here = qkv_weight.shape[1]
    out_cols = heads_here * 3 * HDIM
    piece = lax.all_gather(qkv_weight, "ctx", axis=0, tiled=True)
    qkv = jnp.dot(
        gathered, piece.reshape(piece.shape[0], out_cols), preferred_element_type=jnp.float32
    )
    qkv = qkv.astype(jnp.bfloat16).reshape(group_rows, heads_here, 3, HDIM)
    query = qkv[:, :, 0]
    keys = qkv[:, :, 1]
    values = qkv[:, :, 2]
    inv_root = 1.0 / jnp.sqrt(jnp.float32(HDIM))
    best = jnp.full((heads_here, group_rows), -1e30, jnp.float32)
    key_piece = lax.all_gather(keys, "ctx", axis=0, tiled=True)
    value_piece = lax.all_gather(values, "ctx", axis=0, tiled=True)
    scores = (
        jnp.einsum("qhd,khd->hqk", query, key_piece, preferred_element_type=jnp.float32) * inv_root
    )
    new_best = jnp.maximum(best, jnp.max(scores, -1))
    probs = jnp.exp(scores - new_best[..., None])
    denom = jnp.sum(probs, -1)
    accum = jnp.einsum(
        "hqk,khd->hqd", probs.astype(jnp.bfloat16), value_piece, preferred_element_type=jnp.float32
    )
    best, denom, accum = (new_best, denom, accum)
    result = (accum / denom[..., None]).astype(jnp.bfloat16)
    return result.transpose(1, 0, 2).reshape(group_rows, heads_here * HDIM)


def solution(mesh):
    return jax.shard_map(
        shards,
        mesh=mesh,
        in_specs=(
            P("dp", "head", "ctx"),
            P("dp", "head", "ctx"),
            P(),
            P(),
            P(),
            P(None, ("head", "ctx")),
            P("dp"),
            P(None, ("head", "ctx")),
            P("ctx", "head", None, None),
        ),
        out_specs=P(("dp", "ctx"), "head"),
        check_vma=False,
    )
```

profile of v0, /device:TPU:1, one launch (start us, length us, event | category | flops | bytes accessed | tf_op | source)
XLA Modules:
  0.0 923.7 jit_solution(17581543572212077937)
XLA Ops:
  6.5 0.7 all-gather.8.cloned.1.call-update
  7.3 0.9 constant_dynamic-update-slice_fusion.1
  8.3 1.1 constant_dynamic-update-slice_fusion
  9.4 0.8 reshape.49
  10.1 0.6 fusion.119
  10.8 4.6 collective-permute-start
  15.3 1.3 collective-permute-start.1
  17.4 0.7 dynamic-slice
  19.2 141.1 %all-reduce = f32[10240]{0:T(1024)S(1)} all-reduce(f32[10240]{0:T(1024)S(1)} %dynamic-update-slice), channel_id=1, replica_groups=mesh['dp'=4,'head'=4,'ctx'=8] {'head','ctx'}, use_global_device_ids=true, to_apply=%add | all-reduce | flops 10240 | bytes 81920
  160.4 0.5 slice.249
  162.0 0.8 constant_dynamic-update-slice_fusion.6
  163.4 0.8 constant_dynamic-update-slice_fusion.7
  164.3 1.3 collective-permute-start.2
  165.6 1.5 collective-permute-start.3
  167.6 1.4 collective-permute-done.2
  168.9 1.9 fusion.81
  170.8 1.3 collective-permute-done.3
  172.1 2.1 fusion.73
  174.2 0.9 fusion.13
  175.2 0.9 fusion.25
  176.1 0.9 fusion.31
  176.9 0.9 fusion.43
  177.8 0.9 fusion.49
  178.7 0.9 fusion.19
  179.6 0.9 fusion.37
  180.6 0.9 fusion.55
  181.5 2.6 multiply_convert_fusion
  184.1 0.8 reshape.50
  184.9 0.9 copy.36
  185.8 0.8 reshape.51
  187.7 8.9 all-gather.8.cloned.1.call-done
  196.7 5.9 multiply_reduce_fusion.1
  202.6 1.5 add_convert_fusion
  204.2 0.6 copy-done.2
  204.8 3.1 copy.17
  208.0 63.2 %all-gather.10.cloned.1.call-done = bf16[512,5120]{1,0:T(8,128)(2,1)} async-done(((bf16[128,5120]{1,0:T(8,128)(2,1)}), bf16[512,5120]{1,0:T(8,128)(2,1)}) %all-gather.10.cloned.1.call-update) | async-done | bytes 5242896 | tf_op jit(solution)/shard_map/all_gather | solution.py:92
  271.2 381.9 %all-gather.12.cloned.1.call-done = bf16[5120,5,3,128]{0,3,2,1:T(8,128)(2,1)} async-done(((bf16[640,5,3,128]{0,3,2,1:T(8,128)(2,1)}), bf16[5120,5,3,128]{0,3,2,1:T(8,128)(2,1)}) %all-gather.12.cloned.1.call-update) | async-done | bytes 19660816 | tf_op jit(solution)/shard_map/all_gather | solution.py:96
  653.1 17.7 %convolution_convert_fusion = bf16[512,1920]{1,0:T(8,128)(2,1)} fusion(bf16[512,5120]{1,0:T(8,128)(2,1)} %all-gather.10.cloned.1.call-done, bf16[5120,1920]{0,1:T(8,128)(2,1)} %bitcast.113), kind=kOutput, calls=%fused_computation.24 | convolution fusion | flops 10067312640 | bytes 26869760 | tf_op jit(solution)/shard_map/dot_general | solution.py:97
  670.8 2.7 copy.18
  673.5 1.0 fusion.115
  674.5 1.1 copy.33
  675.6 0.5 all-gather.16.cloned.1.call-update
  676.2 110.6 %all-gather.14.cloned.1.call-done = bf16[4096,5,1,128]{3,0,1,2:T(8,128)(2,1)} async-done(((bf16[512,5,1,128]{3,0,1,2:T(8,128)(2,1)}), bf16[4096,5,1,128]{3,0,1,2:T(8,128)(2,1)}) %all-gather.14.cloned.1.call-update) | async-done | bytes 5242896 | tf_op jit(solution)/shard_map/all_gather | solution.py:106
  786.8 19.0 %multiply_reduce_fusion = (f32[5,512]{1,0:T(8,128)S(1)}, f32[5,512,4096]{2,1,0:T(8,128)}) fusion(bf16[4096,5,1,128]{3,0,1,2:T(8,128)(2,1)} %all-gather.14.cloned.1.call-done, bf16[512,5,3,128]{0,3,2,1:T(8,128)(2,1)S(1)} %bitcast.108), kind=kOutput, calls=%fused_computation.1 | convolution fusion | flops 2705323520 | bytes 47851520 | tf_op jit(solution)/shard_map/qhd,khd->hqk/dot_general | solution.py:109
  805.8 17.3 %fusion = f32[5,512]{1,0:T(8,128)S(1)} fusion(f32[5,512,4096]{2,1,0:T(8,128)} %get-tuple-element.47, f32[5,512]{1,0:T(8,128)S(1)} %broadcast_maximum_fusion), kind=kLoop, calls=%fused_computation.2 | loop fusion | flops 31454720 | bytes 41963520 | tf_op jit(solution)/shard_map/reduce_sum | solution.py:113
  823.2 75.6 %all-gather.16.cloned.1.call-done = bf16[4096,5,1,128]{0,3,1,2:T(8,128)(2,1)} async-done(((bf16[512,5,1,128]{0,3,1,2:T(8,128)(2,1)}), bf16[4096,5,1,128]{0,3,1,2:T(8,128)(2,1)}) %all-gather.16.cloned.1.call-update) | async-done | bytes 5242896 | tf_op jit(solution)/shard_map/all_gather | solution.py:107
  898.7 17.3 %divide_convert_fusion = bf16[512,5,128]{0,2,1:T(8,128)(2,1)S(1)} fusion(bf16[4096,5,1,128]{0,3,1,2:T(8,128)(2,1)} %all-gather.16.cloned.1.call-done, f32[5,512,4096]{2,1,0:T(8,128)} %get-tuple-element.47, f32[5,512]{1,0:T(8,128)S(1)} %broadcast_maximum_fusion, f32[512,5]{0,1:T(8,128)S(1)} %bitcast.112), kind=kOutput, calls=%fused_computation.84 | convolution fusion | flops 2716467200 | bytes 47861760 | tf_op jit(solution)/shard_map/hqk,khd->hqd/dot_general | solution.py:114
  916.1 1.1 copy.22
  (46 shorter events, 4.1 us)
Async XLA Ops:
  6.5 180.0 %copy-start = (bf16[768,192]{0,1:T(8,128)(2,1)S(1)}, bf16[768,192]{0,1:T(8,128)(2,1)}, u32[]{:S(2)}) copy-start(bf16[768,192]{0,1:T(8,128)(2,1)} %param.13) | copy-start | bytes 884740
  6.5 10.8 %copy-start.7 = (u32[128]{0:T(128)S(1)}, u32[128]{0:T(128)}, u32[]{:S(2)}) copy-start(u32[128]{0:T(128)} %constant.27) | copy-start | bytes 1540
  6.5 12.2 %copy-start.4 = (bf16[256,320]{0,1:T(8,128)(2,1)S(1)}, bf16[256,320]{0,1:T(8,128)(2,1)}, u32[]{:S(2)}) copy-start(bf16[256,320]{0,1:T(8,128)(2,1)} %param.16) | copy-start | bytes 491524
  6.5 190.1 %all-gather.8.cloned.1.call-start = ((), (), s32[]{:S(2)}) async-start(), calls=%async_computation | async-start | bytes 8110080 | tf_op jit(solution)/shard_map/all_gather | solution.py:87
  7.3 264.0 %all-gather.10.cloned.1.call-start = ((), (), s32[]{:S(2)}) async-start(), calls=%async_computation.1 | async-start | bytes 6553600 | tf_op jit(solution)/shard_map/all_gather | solution.py:92
  8.3 152.2 %copy-start.3 = (bf16[4,16,3072]{2,1,0:T(8,128)(2,1)S(1)}, bf16[4,16,3072]{2,1,0:T(8,128)(2,1)}, u32[]{:S(2)}) copy-start(bf16[4,16,3072]{2,1,0:T(8,128)(2,1)} %param.9) | copy-start | bytes 1179652
  10.8 151.3 %collective-permute-start = (bf16[6,1,32,96]{3,2,1,0:T(8,128)(2,1)}, bf16[6,1,32,96]{3,2,1,0:T(8,128)(2,1)}, u32[]{:S(2)}, u32[]{:S(2)}) collective-permute-start(bf16[6,1,32,96]{3,2,1,0:T(8,128)(2,1)} %get-tuple-element.35), channel_id=1, source_target_pairs={{0,8},{8,16},{16,24},{1,9},{9,17},{17,25},{2,10},{10,18},{18,26},{... | collective-permute-start | bytes 110600 | tf_op jit(solution)/shard_map/ppermute | solution.py:19
  15.3 148.0 %collective-permute-start.1 = (bf16[6,1,32,96]{3,2,1,0:T(8,128)(2,1)}, bf16[6,1,32,96]{3,2,1,0:T(8,128)(2,1)}, u32[]{:S(2)}, u32[]{:S(2)}) collective-permute-start(bf16[6,1,32,96]{3,2,1,0:T(8,128)(2,1)} %get-tuple-element.34), channel_id=1, source_target_pairs={{8,0},{16,8},{24,16},{9,1},{17,9},{25,17},{10,2},{18,10},{26,18},{... | collective-permute-start | bytes 110600 | tf_op jit(solution)/shard_map/ppermute | solution.py:21
  164.3 4.6 collective-permute-start.2
  165.6 6.5 collective-permute-start.3
  170.8 3.4 copy-start.5
  180.5 0.9 copy-start.6
  202.6 2.2 copy-start.2
  204.1 449.0 %all-gather.12.cloned.1.call-start = ((), (), s32[]{:S(2)}) async-start(), calls=%async_computation.2 | async-start | bytes 22118400 | tf_op jit(solution)/shard_map/all_gather | solution.py:96
  207.9 578.8 %all-gather.14.cloned.1.call-start = ((), (), s32[]{:S(2)}) async-start(), calls=%async_computation.3 | async-start | bytes 5898240 | tf_op jit(solution)/shard_map/all_gather | solution.py:106
  675.6 223.2 %all-gather.16.cloned.1.call-start = ((), (), s32[]{:S(2)}) async-start(), calls=%async_computation.4 | async-start | bytes 5898240 | tf_op jit(solution)/shard_map/all_gather | solution.py:107
  898.7 18.4 %copy-start.1 = (bf16[768,192]{0,1:T(8,128)(2,1)S(1)}, bf16[768,192]{0,1:T(8,128)(2,1)}, u32[]{:S(2)}) copy-start(bf16[768,192]{0,1:T(8,128)(2,1)} %param.13) | copy-start | bytes 884740
Sparse Core Ops, SparseCore 0:
  9.0 187.6 all-gather.7
  204.2 66.9 all-gather.9
  272.9 380.1 all-gather.11
  675.7 111.0 all-gather.13
  788.3 110.4 all-gather.15
where the time goes:
time: 924 us
  waiting for transfers between devices  644 us (70%)
  blocking collectives  141 us (15%)
  matrix products  70.4 us (8%)
  other arithmetic  22.9 us (2%)
  local copies, waits for them, and re-layouts  21.4 us (2%)
  between operations  14.9 us (2%)
    all_gather x1, waiting for transfers between devices, shards(): piece = lax.all_gather(qkv_weight, 'ctx', axis=0, tiled=True)  382 us
    unnamed x1, blocking collectives  141 us
    all_gather x1, waiting for transfers between devices, shards(): key_piece = lax.all_gather(keys, 'ctx', axis=0, tiled=True)  111 us
    all_gather x1, waiting for transfers between devices, shards(): value_piece = lax.all_gather(values, 'ctx', axis=0, tiled=True)  75.6 us
    all_gather x1, waiting for transfers between devices, shards(): gathered = lax.all_gather(normed, 'head', axis=0, tiled=True)  63.2 us
    dot_general x1, matrix products, shards(): jnp.einsum('qhd,khd->hqk', query, key_piece, preferred_element_type=jnp.f...  19 us
  transfers between devices with their start and end apart: 9, of which 7 were waited for; matrix products, arithmetic and copies ran while one was open for 7% of the time, Pallas kernels for 0%

commit v1 on v0

--- a/solution.py
+++ b/solution.py
@@ -103,8 +103,11 @@
     values = qkv[:, :, 2]
     inv_root = 1.0 / jnp.sqrt(jnp.float32(HDIM))
     best = jnp.full((heads_here, group_rows), -1e30, jnp.float32)
-    key_piece = lax.all_gather(keys, "ctx", axis=0, tiled=True)
-    value_piece = lax.all_gather(values, "ctx", axis=0, tiled=True)
+    key_piece, value_piece = jnp.split(
+        lax.all_gather(jnp.concatenate([keys, values], axis=1), "ctx", axis=0, tiled=True),
+        [keys.shape[1]],
+        axis=1,
+    )
     scores = (
         jnp.einsum("qhd,khd->hqk", query, key_piece, preferred_element_type=jnp.float32) * inv_root
     )

time: 924 us -> 953 us (1.031)
  waiting for transfers between devices: 644 us -> 670 us
    all_gather x2 -> x1, waiting for transfers between devices: 186 us -> 209 us  [shards(): lax.all_gather(jnp.concatenate([keys, values], axis=1), 'ctx', axis=0, ti...]
  transfers between devices with their start and end apart: 9 -> 8, of which waited for: 7 -> 5; matrix products, arithmetic and copies ran while one was open for 7% -> 3% of each run, Pallas kernels for 0% -> 0%
where the time goes in v1:
time: 953 us; the launch traced here: 952 us
  waiting for transfers between devices  670 us (70%)
  blocking collectives  138 us (14%)
  matrix products  70.9 us (7%)
  other arithmetic  25.2 us (3%)
  local copies, waits for them, and re-layouts  24.1 us (3%)
  between operations  14.8 us (2%)
    all_gather x1, waiting for transfers between devices, shards(): piece = lax.all_gather(qkv_weight, 'ctx', axis=0, tiled=True)  382 us
    all_gather x1, waiting for transfers between devices, shards(): lax.all_gather(jnp.concatenate([keys, values], axis=1), 'ctx', axis=0, ti...  209 us
    unnamed x1, blocking collectives  138 us
    all_gather x1, waiting for transfers between devices, shards(): gathered = lax.all_gather(normed, 'head', axis=0, tiled=True)  63.6 us
  transfers between devices with their start and end apart: 8, of which 5 were waited for; matrix products, arithmetic and copies ran while one was open for 3% of the time, Pallas kernels for 0%

profile of v1, /device:TPU:1, one launch (start us, length us, event | category | flops | bytes accessed | tf_op | source)
XLA Modules:
  0.0 951.8 jit_solution(2672845709657614051)
XLA Ops:
  6.5 0.7 all-gather.5.cloned.1.call-update
  7.3 0.9 constant_dynamic-update-slice_fusion.1
  8.3 1.1 constant_dynamic-update-slice_fusion
  9.4 0.8 reshape.49
  10.1 0.6 fusion.119
  10.8 1.3 collective-permute-start.1
  12.1 5.2 collective-permute-start
  18.0 0.6 dynamic-slice
  19.7 137.9 %all-reduce = f32[10240]{0:T(1024)S(1)} all-reduce(f32[10240]{0:T(1024)S(1)} %dynamic-update-slice), channel_id=1, replica_groups=mesh['dp'=4,'head'=4,'ctx'=8] {'head','ctx'}, use_global_device_ids=true, to_apply=%add | all-reduce | flops 10240 | bytes 81920
  157.7 0.5 slice.249
  158.2 0.5 slice.224
  159.3 0.8 constant_dynamic-update-slice_fusion.6
  160.6 0.8 constant_dynamic-update-slice_fusion.7
  161.5 1.3 collective-permute-start.2
  162.8 1.5 collective-permute-start.3
  164.8 4.4 collective-permute-done.3
  169.3 2.2 fusion.73
  171.5 1.9 fusion.81
  173.4 0.9 fusion.19
  174.3 0.9 fusion.13
  175.2 0.9 fusion.25
  176.1 0.9 fusion.31
  177.0 0.9 fusion.37
  177.9 0.9 fusion.43
  178.8 0.9 fusion.49
  179.7 0.9 fusion.55
  180.6 2.6 multiply_convert_fusion
  183.3 0.8 reshape.50
  184.1 0.9 copy.39
  184.9 0.8 reshape.51
  186.9 10.2 %all-gather.5.cloned.1.call-done = bf16[768,5120]{0,1:T(8,128)(2,1)} async-done(((bf16[768,160]{0,1:T(8,128)(2,1)}), bf16[768,5120]{0,1:T(8,128)(2,1)}) %all-gather.5.cloned.1.call-update) | async-done | bytes 7864336 | tf_op jit(solution)/shard_map/all_gather | solution.py:87
  197.0 5.9 multiply_reduce_fusion.1
  203.0 1.5 add_convert_fusion
  204.6 0.6 copy-done.2
  205.2 3.1 copy.18
  208.4 63.6 %all-gather.7.cloned.1.call-done = bf16[512,5120]{1,0:T(8,128)(2,1)} async-done(((bf16[128,5120]{1,0:T(8,128)(2,1)}), bf16[512,5120]{1,0:T(8,128)(2,1)}) %all-gather.7.cloned.1.call-update) | async-done | bytes 5242896 | tf_op jit(solution)/shard_map/all_gather | solution.py:92
  271.9 381.9 %all-gather.9.cloned.1.call-done = bf16[5120,5,3,128]{0,3,2,1:T(8,128)(2,1)} async-done(((bf16[640,5,3,128]{0,3,2,1:T(8,128)(2,1)}), bf16[5120,5,3,128]{0,3,2,1:T(8,128)(2,1)}) %all-gather.9.cloned.1.call-update) | async-done | bytes 19660816 | tf_op jit(solution)/shard_map/all_gather | solution.py:96
  653.8 17.7 %convolution_convert_fusion = bf16[512,1920]{1,0:T(8,128)(2,1)} fusion(bf16[512,5120]{1,0:T(8,128)(2,1)} %all-gather.7.cloned.1.call-done, bf16[5120,1920]{0,1:T(8,128)(2,1)} %bitcast.103), kind=kOutput, calls=%fused_computation.24 | convolution fusion | flops 10067312640 | bytes 26869760 | tf_op jit(solution)/shard_map/dot_general | solution.py:97
  671.6 2.7 copy.19
  674.3 1.2 fusion.115
  675.5 1.4 copy.36
  676.9 2.2 copy.37
  679.1 2.3 pad_maximum_fusion.2
  681.4 208.8 %all-gather.11.cloned.1.call-done = bf16[4096,10,128]{2,0,1:T(8,128)(2,1)} async-done(((bf16[512,10,128]{2,0,1:T(8,128)(2,1)}), bf16[4096,10,128]{2,0,1:T(8,128)(2,1)}) %all-gather.11.cloned.1.call-update) | async-done | bytes 10485776 | tf_op jit(solution)/shard_map/all_gather | solution.py:107
  890.2 18.8 %multiply_reduce_fusion = (f32[5,512]{1,0:T(8,128)S(1)}, f32[5,512,4096]{2,1,0:T(8,128)}) fusion(bf16[4096,10,128]{2,0,1:T(8,128)(2,1)} %all-gather.11.cloned.1.call-done, bf16[512,5,3,128]{0,3,2,1:T(8,128)(2,1)S(1)} %bitcast.96), kind=kOutput, calls=%fused_computation.1 | convolution fusion | flops 2705323520 | bytes 47851520 | tf_op jit(solution)/shard_map/qhd,khd->hqk/dot_general | solution.py:112
  909.0 17.2 %fusion = f32[5,512]{1,0:T(8,128)S(1)} fusion(f32[5,512,4096]{2,1,0:T(8,128)} %get-tuple-element.47, f32[5,512]{1,0:T(8,128)S(1)} %broadcast_maximum_fusion), kind=kLoop, calls=%fused_computation.2 | loop fusion | flops 31454720 | bytes 41963520 | tf_op jit(solution)/shard_map/reduce_sum | solution.py:116
  926.2 18.0 %divide_convert_fusion = bf16[512,5,128]{0,2,1:T(8,128)(2,1)S(1)} fusion(bf16[4096,10,128]{2,0,1:T(8,128)(2,1)} %all-gather.11.cloned.1.call-done, f32[5,512,4096]{2,1,0:T(8,128)} %get-tuple-element.47, f32[5,512]{1,0:T(8,128)S(1)} %broadcast_maximum_fusion, f32[512,5]{0,1:T(8,128)S(1)} %bitcast.102), kind=kOutput, calls=%fused_computation.85 | convolution fusion | flops 2716467200 | bytes 47861760 | tf_op jit(solution)/shard_map/hqk,khd->hqd/dot_general | solution.py:117
  944.2 1.1 copy.24
  (45 shorter events, 3.6 us)
Async XLA Ops:
  6.5 179.2 %copy-start = (bf16[768,192]{0,1:T(8,128)(2,1)S(1)}, bf16[768,192]{0,1:T(8,128)(2,1)}, u32[]{:S(2)}) copy-start(bf16[768,192]{0,1:T(8,128)(2,1)} %param.13) | copy-start | bytes 884740
  6.5 11.5 %copy-start.7 = (u32[128]{0:T(128)S(1)}, u32[128]{0:T(128)}, u32[]{:S(2)}) copy-start(u32[128]{0:T(128)} %constant.27) | copy-start | bytes 1540
  6.5 12.6 %copy-start.4 = (bf16[256,320]{0,1:T(8,128)(2,1)S(1)}, bf16[256,320]{0,1:T(8,128)(2,1)}, u32[]{:S(2)}) copy-start(bf16[256,320]{0,1:T(8,128)(2,1)} %param.16) | copy-start | bytes 491524
  6.5 190.5 %all-gather.5.cloned.1.call-start = ((), (), s32[]{:S(2)}) async-start(), calls=%async_computation | async-start | bytes 8110080 | tf_op jit(solution)/shard_map/all_gather | solution.py:87
  7.3 264.7 %all-gather.7.cloned.1.call-start = ((), (), s32[]{:S(2)}) async-start(), calls=%async_computation.1 | async-start | bytes 6553600 | tf_op jit(solution)/shard_map/all_gather | solution.py:92
  8.3 149.4 %copy-start.3 = (bf16[4,16,3072]{2,1,0:T(8,128)(2,1)S(1)}, bf16[4,16,3072]{2,1,0:T(8,128)(2,1)}, u32[]{:S(2)}) copy-start(bf16[4,16,3072]{2,1,0:T(8,128)(2,1)} %param.9) | copy-start | bytes 1179652
  10.8 149.8 %collective-permute-start.1 = (bf16[6,1,32,96]{3,2,1,0:T(8,128)(2,1)}, bf16[6,1,32,96]{3,2,1,0:T(8,128)(2,1)}, u32[]{:S(2)}, u32[]{:S(2)}) collective-permute-start(bf16[6,1,32,96]{3,2,1,0:T(8,128)(2,1)} %get-tuple-element.34), channel_id=1, source_target_pairs={{8,0},{16,8},{24,16},{9,1},{17,9},{25,17},{10,2},{18,10},{26,18},{... | collective-permute-start | bytes 110600 | tf_op jit(solution)/shard_map/ppermute | solution.py:21
  12.1 147.2 %collective-permute-start = (bf16[6,1,32,96]{3,2,1,0:T(8,128)(2,1)}, bf16[6,1,32,96]{3,2,1,0:T(8,128)(2,1)}, u32[]{:S(2)}, u32[]{:S(2)}) collective-permute-start(bf16[6,1,32,96]{3,2,1,0:T(8,128)(2,1)} %get-tuple-element.35), channel_id=1, source_target_pairs={{0,8},{8,16},{16,24},{1,9},{9,17},{17,25},{2,10},{10,18},{18,26},{... | collective-permute-start | bytes 110600 | tf_op jit(solution)/shard_map/ppermute | solution.py:19
  161.5 10.0 %collective-permute-start.2 = (bf16[6,18,1,96]{3,2,1,0:T(2,128)(2,1)S(1)}, bf16[6,18,1,96]{3,2,1,0:T(2,128)(2,1)S(1)}, u32[]{:S(2)}, u32[]{:S(2)}) collective-permute-start(bf16[6,18,1,96]{3,2,1,0:T(2,128)(2,1)S(1)} %get-tuple-element.23), channel_id=1, source_target_pairs={{0,1},{1,2},{2,3},{3,4},{4,5},{5,6},{6,7},{8,9},{9,10},{10,11},{11... | collective-permute-start | bytes 62216 | tf_op jit(solution)/shard_map/ppermute | solution.py:19
  162.8 6.5 collective-permute-start.3
  171.5 1.9 copy-start.5
  179.7 0.9 copy-start.6
  203.0 2.2 copy-start.2
  204.5 449.3 %all-gather.9.cloned.1.call-start = ((), (), s32[]{:S(2)}) async-start(), calls=%async_computation.2 | async-start | bytes 22118400 | tf_op jit(solution)/shard_map/all_gather | solution.py:96
  208.3 681.9 %all-gather.11.cloned.1.call-start = ((), (), s32[]{:S(2)}) async-start(), calls=%async_computation.3 | async-start | bytes 11796480 | tf_op jit(solution)/shard_map/all_gather | solution.py:107
  926.2 19.1 %copy-start.1 = (bf16[768,192]{0,1:T(8,128)(2,1)S(1)}, bf16[768,192]{0,1:T(8,128)(2,1)}, u32[]{:S(2)}) copy-start(bf16[768,192]{0,1:T(8,128)(2,1)} %param.13) | copy-start | bytes 884740
Sparse Core Ops, SparseCore 0:
  9.0 187.9 all-gather.4
  204.6 67.2 all-gather.6
  273.6 380.1 all-gather.8
  681.5 208.6 all-gather.10
